TPU v7x, 512 devices: a whole 4x8x8 slice. The times are simulated.
512 devices in a mesh: section: 8 (over z), kv: 64 (over x, y, core).
Axes of the slice: x: 4, y: 8, z: 8, core: 2. Of those that a mesh axis runs over, the one named last changes fastest.
Arguments:
- held: bfloat16 [8, 128, 8192], P('section', None, 'kv'), may hold values from -6 to 6
- fresh: bfloat16 [1, 128, 8192], P(None, None, 'kv'), may hold values from -6 to 6
- block_starts: int32 [8], replicated, may hold values from 12288 to 24576
- fresh_starts: int32 [1], replicated, may hold values from 12288 to 24576
- norm_gain: float32 [8, 8192], P('section'), may hold values from 0.25 to 1.75
- w_qkv: bfloat16 [8, 8192, 5120], P('section', None, 'kv'), may hold values from -0.0625 to 0.0625
- w_out: bfloat16 [8, 4096, 8192], P('section', None, 'kv'), may hold values from -12 to 12
- cache_keys: bfloat16 [8, 24576, 512], P('section', 'kv'), may hold values from -400 to 400
- cache_values: bfloat16 [8, 24576, 512], P('section', 'kv'), may hold values from -6 to 6
- cache_lengths: int32 [8, 64], P('section', 'kv'), may hold values from 96 to 384, as said below
Outputs:
- produced: bfloat16 [8, 2, 128, 8192], P('section', None, None, 'kv')
Inputs may be any that keep to these rules, and one draw needn't show every extreme that they name: `cache_lengths`: each section has one block filled to 384.
All inputs are finite; a program needn't handle non-finite values.
Results may differ from a plain program's by a relative error of at most 0.017.
The roundings to bfloat16 on the way count: a program that leaves them out, or rounds other values in their place, can miss the bound.
Values may be sent and summed in bfloat16 or wider, within the bound.
No kernel may reach another device: no remote copies, remote signals or barrier semaphores. Data moves between devices by JAX's collectives and lax.ppermute only.
A program may use at most 128 MiB of HBM per device.

v0:
```python
import jax
import jax.numpy as jnp
from jax import lax
from jax.sharding import PartitionSpec as P

HD = 128
HEADS_Q = 32
KV_HEADS = 4


def passed_along(block, axis, distance):
    devices = range(lax.axis_size(axis))
    route = [(i - distance, i) for i in devices if i - distance in devices]
    return lax.ppermute(block, axis, route)


def block_partial(query, key_rows, value_rows, valid):
    row_count = query.shape[0]
    head_count = query.shape[1]
    head_width = query.shape[2]
    group_count = key_rows.shape[1]
    group_size = head_count // group_count
    shaped = jnp.transpose(
        query.reshape(row_count, group_count, group_size, head_width), (1, 0, 2, 3)
    )
    key_major = jnp.transpose(key_rows, (1, 0, 2))
    value_major = jnp.transpose(value_rows, (1, 0, 2))
    allowed = valid[:, None, :]

    def one_group(packed):
        group_query, group_keys, group_values = packed
        scores = jnp.einsum(
            "tgd,id->tgi", group_query, group_keys, preferred_element_type=jnp.float32
        ) * head_width ** (-0.5)
        row_max = jnp.max(jnp.where(allowed, scores, -1e30), axis=2)
        expo = jnp.where(allowed, jnp.exp(scores - row_max[..., None]), 0.0)
        row_sum = jnp.sum(expo, axis=2)
        weights = expo.astype(jnp.bfloat16)
        weighted = jnp.einsum(
            "tgi,id->tgd", weights, group_values, preferred_element_type=jnp.float32
        )
        return (row_max, row_sum, weighted)

    maxima, totals, sums = lax.map(one_group, (shaped, key_major, value_major))
    maxima = jnp.transpose(maxima, (1, 0, 2)).reshape(row_count, head_count)
    totals = jnp.transpose(totals, (1, 0, 2)).reshape(row_count, head_count)
    sums = jnp.transpose(sums, (1, 0, 2, 3)).reshape(row_count, head_count * head_width)
    return (maxima, totals, sums)


def combine_two(left_part, right_part):
    head_count = left_part[0].shape[1]
    row_count = left_part[0].shape[0]
    overall = jnp.maximum(left_part[0], right_part[0])
    left_factor = jnp.exp(left_part[0] - overall)
    right_factor = jnp.exp(right_part[0] - overall)
    total = left_part[1] * left_factor + right_part[1] * right_factor
    left_sum = left_part[2].reshape(row_count, head_count, -1) * left_factor[..., None]
    right_sum = right_part[2].reshape(row_count, head_count, -1) * right_factor[..., None]
    return (overall, total, (left_sum + right_sum).reshape(row_count, -1))


def merge_stack(maxima, totals, sums):
    count = maxima.shape[0]
    row_count = maxima.shape[1]
    head_count = maxima.shape[2]
    overall = jnp.max(maxima, axis=0)
    factor = jnp.exp(maxima - overall)
    total = jnp.sum(totals * factor, axis=0)
    summed = jnp.sum(sums.reshape(count, row_count, head_count, -1) * factor[..., None], axis=0)
    return (summed / total[..., None]).reshape(row_count, -1).astype(jnp.bfloat16)


def on_device(
    held,
    fresh,
    block_starts,
    fresh_starts,
    norm_gain,
    w_qkv,
    w_out,
    cache_keys,
    cache_values,
    cache_lengths,
):
    kv_index = lax.axis_index("kv")
    section_index = lax.axis_index("section")
    tick_count = fresh.shape[0] + 1
    row_count = held.shape[1]
    slot_count = cache_keys.shape[1]
    key_rows = cache_keys[0].reshape(slot_count, KV_HEADS, HD)
    value_rows = cache_values[0].reshape(slot_count, KV_HEADS, HD)
    filled = cache_lengths[0, 0]
    gain = norm_gain[0]
    weight_in = w_qkv[0]
    weight_out = w_out[0]
    slot_ids = jnp.arange(slot_count, dtype=jnp.int32)
    positions = kv_index * slot_count + slot_ids
    row_ids = jnp.arange(row_count, dtype=jnp.int32)
    causal = row_ids[None, :] <= row_ids[:, None]
    current = held[0]
    results = []
    for tick_index in range(tick_count):
        if tick_index > 0:
            passed = passed_along(current, "section", 1)
            current = jnp.where(section_index == 0, fresh[tick_index - 1], passed)
        anchor = section_index - tick_index
        start = jnp.where(
            anchor >= 0,
            block_starts[jnp.maximum(anchor, 0)],
            fresh_starts[jnp.clip(-anchor - 1, 0, tick_count - 2)],
        )
        gathered = lax.all_gather(current, "kv", axis=1, tiled=True)
        wide = gathered.astype(jnp.float32)
        normed = (
            wide * lax.rsqrt(jnp.mean(wide * wide, axis=1, keepdims=True) + 1e-05) * gain
        ).astype(jnp.bfloat16)
        local_cols = jnp.dot(normed, weight_in, preferred_element_type=jnp.float32).astype(
            jnp.bfloat16
        )
        united = lax.all_gather(local_cols, "kv", axis=1, tiled=True)
        query = united[:, : HEADS_Q * HD].reshape(row_count, HEADS_Q, HD)
        new_keys = united[:, HEADS_Q * HD : (HEADS_Q + KV_HEADS) * HD].reshape(
            row_count, KV_HEADS, HD
        )
        new_values = united[:, (HEADS_Q + KV_HEADS) * HD :].reshape(row_count, KV_HEADS, HD)
        usable = (slot_ids < filled) & (positions < start)
        valid = jnp.broadcast_to(usable[None, :], (row_count, slot_count))
        partial_value = block_partial(query, key_rows, value_rows, valid)

        def with_own(parts):
            return combine_two(parts, block_partial(query, new_keys, new_values, causal))

        def without_own(parts):
            return parts

        partial_value = lax.cond(kv_index == 0, with_own, without_own, partial_value)
        received = (
            lax.all_to_all(partial_value[0][None], "kv", split_axis=1, concat_axis=0, tiled=True),
            lax.all_to_all(partial_value[1][None], "kv", split_axis=1, concat_axis=0, tiled=True),
            lax.all_to_all(partial_value[2][None], "kv", split_axis=1, concat_axis=0, tiled=True),
        )
        attended = merge_stack(received[0], received[1], received[2])
        branch = jnp.dot(
            lax.all_gather(attended, "kv", axis=0, tiled=True),
            weight_out,
            preferred_element_type=jnp.float32,
        )
        current = (current.astype(jnp.float32) + branch).astype(jnp.bfloat16)
        results.append(current)
    return jnp.stack(results, 0)[None]


def solution(mesh):
    in_specs = (
        P("section", None, "kv"),
        P(None, None, "kv"),
        P(),
        P(),
        P("section", None),
        P("section", None, "kv"),
        P("section", None, "kv"),
        P("section", "kv", None),
        P("section", "kv", None),
        P("section", "kv"),
    )
    out_specs = P("section", None, None, "kv")
    return jax.shard_map(
        on_device, mesh=mesh, in_specs=in_specs, out_specs=out_specs, check_vma=False
    )
```

profile of v0, /device:TPU:1, one launch (start us, length us, event | category | flops | bytes accessed | tf_op | source)
XLA Modules:
  0.0 792.7 jit_solution(17048475888363732458)
XLA Ops:
  7.3 86.4 %all-gather.16.cloned.1.call-done = bf16[1,128,8192]{2,1,0:T(8,128)(2,1)} async-done(((bf16[1,128,128]{2,1,0:T(8,128)(2,1)}), bf16[1,128,8192]{2,1,0:T(8,128)(2,1)}) %all-gather.16.cloned.1.call-update) | async-done | bytes 2097168 | tf_op jit(solution)/shard_map/all_gather | solution.py:113
  93.7 2.2 fusion.77
  96.0 1.6 fusion.97
  97.9 0.9 copy.78
  99.0 0.9 copy.79
  103.6 75.6 %all-gather.10.cloned.1.call-done = bf16[128,5120]{0,1:T(8,128)(2,1)} async-done(((bf16[128,80]{0,1:T(8,128)(2,1)}), bf16[128,5120]{0,1:T(8,128)(2,1)}) %all-gather.10.cloned.1.call-update) | async-done | bytes 1310736 | tf_op jit(solution)/shard_map/all_gather | solution.py:121
  179.2 1.3 slice.24
  180.6 1.3 copy.75
  182.1 13.5 %while.58 = (s32[]{:T(128)}, f32[4,128,8]{1,2,0:T(8,128)S(1)}, f32[4,128,8]{1,2,0:T(8,128)S(1)}, f32[4,128,8,128]{3,1,2,0:T(8,128)S(1)}, bf16[4,128,8,128]{3,1,2...) while((s32[]{:T(128)}, f32[4,128,8]{1,2,0:T(8,128)S(1)}, ...), condition=%wide.region_4.5_spmd.clone, body=%wide.region_1.4_spmd.clone.sunk | while | flops 204863488 | bytes 5737833 | solution.py:44
  182.1 1.5 select_reduce_fusion.8
  184.1 1.3 fusion.142
  185.5 1.5 select_reduce_fusion.8
  187.5 1.3 fusion.142
  188.9 1.5 select_reduce_fusion.8
  190.9 1.3 fusion.142
  192.2 1.5 select_reduce_fusion.8
  194.2 1.3 fusion.142
  195.6 12.1 %conditional.2 = (f32[128,32]{0,1:T(8,128)S(1)}, f32[128,32]{0,1:T(8,128)S(1)}, f32[128,4096]{1,0:T(8,128)}) conditional(s32[]{:T(128)} %convert_element_type.53, (f32[128,4,8,128]{3,0,2,1:T(8,128)S(1)}, f32[128,32]{0,1:T(8,128)S(1)}, f32[128,32]{0,1:T(8,128)S(1)}) %tuple.192, (bf16[128,4096]{0,1:T(8,128)(2,1)}, bf16[128,5120]{0,1:T(8,128)(2,1)}, ...), branch_computations={%region_5.6_spmd, %region_6.11_spmd} | conditional | flops 69883904 | bytes 51759524 | solution.py:137
  195.6 1.2 copy.80
  196.8 3.0 copy.131
  207.7 0.7 copy.83
  208.4 25.7 %all-to-all-start.2 = ((f32[1,128,32]{2,0,1:T(1,128)}), f32[1,128,32]{2,0,1:T(1,128)S(1)}, u32[]{:S(2)}, u32[]{:S(2)}) async-start(f32[1,128,32]{2,0,1:T(1,128)} %bitcast.73), calls=%async_computation.2 | async-start | bytes 131072 | tf_op jit(solution)/shard_map/all_to_all | solution.py:140
  234.1 0.7 copy.82
  234.8 9.2 %all-to-all-done.2 = f32[1,128,32]{2,0,1:T(1,128)S(1)} async-done(((f32[1,128,32]{2,0,1:T(1,128)}), f32[1,128,32]{2,0,1:T(1,128)S(1)}, u32[]{:S(2)}, u32[]{:S(2)}) %all-to-all-start.2) | async-done | bytes 16416 | tf_op jit(solution)/shard_map/all_to_all | solution.py:140
  244.0 4.4 all-to-all-start.1
  248.4 5.3 broadcast_in_dim.169
  253.8 4.5 all-to-all-done.1
  258.3 5.9 all-to-all-start
  264.9 0.9 multiply_reduce_fusion.3
  265.9 49.5 %all-to-all-done = f32[1,128,4096]{2,0,1:T(1,128)S(1)} async-done(((f32[1,128,4096]{2,0,1:T(1,128)}), f32[1,128,4096]{2,0,1:T(1,128)S(1)}, u32[]{:S(2)}, u32[]{:S(2)}) %all-to-all-start) | async-done | bytes 2097184 | tf_op jit(solution)/shard_map/all_to_all | solution.py:141
  316.0 4.3 multiply_reduce_fusion.1
  321.1 79.2 %all-gather.18.cloned.1.call-done = bf16[64,2,4096]{2,1,0:T(2,128)(2,1)} async-done(((bf16[1,2,4096]{2,1,0:T(2,128)(2,1)}), bf16[64,2,4096]{2,1,0:T(2,128)(2,1)}) %all-gather.18.cloned.1.call-update) | async-done | bytes 1048592 | tf_op jit(solution)/shard_map/all_gather | solution.py:145
  400.3 1.5 reshape.190
  402.2 3.3 collective-permute-start
  405.5 1.0 collective-permute-done
  407.3 78.1 %all-gather.12.cloned.1.call-done = bf16[128,8192]{1,0:T(8,128)(2,1)} async-done(((bf16[128,128]{1,0:T(8,128)(2,1)}), bf16[128,8192]{1,0:T(8,128)(2,1)}) %all-gather.12.cloned.1.call-update) | async-done | bytes 2097168 | tf_op jit(solution)/shard_map/all_gather | solution.py:113
  485.5 2.2 fusion.74
  487.7 1.6 fusion.92
  489.4 81.6 %all-gather.14.cloned.1.call-done = bf16[128,5120]{0,1:T(8,128)(2,1)} async-done(((bf16[128,80]{0,1:T(8,128)(2,1)}), bf16[128,5120]{0,1:T(8,128)(2,1)}) %all-gather.14.cloned.1.call-update) | async-done | bytes 1310736 | tf_op jit(solution)/shard_map/all_gather | solution.py:121
  571.0 1.3 slice.25
  572.3 1.3 copy.84
  573.9 13.5 %while.59 = (s32[]{:T(128)}, f32[4,128,8]{1,2,0:T(8,128)S(1)}, f32[4,128,8]{1,2,0:T(8,128)S(1)}, f32[4,128,8,128]{3,1,2,0:T(8,128)S(1)}, bf16[4,128,8,128]{3,1,2...) while((s32[]{:T(128)}, f32[4,128,8]{1,2,0:T(8,128)S(1)}, ...), condition=%wide.region_18.19_spmd.clone, body=%wide.region_15.18_spmd.clone.sunk | while | flops 204863488 | bytes 5737833 | solution.py:44
  573.9 1.5 select_reduce_fusion.9
  575.9 1.3 fusion.146
  577.3 1.5 select_reduce_fusion.9
  579.3 1.3 fusion.146
  580.6 1.5 select_reduce_fusion.9
  582.6 1.3 fusion.146
  584.0 1.5 select_reduce_fusion.9
  586.0 1.3 fusion.146
  587.4 4.4 conditional.3
  587.4 1.2 copy.87
  588.6 3.0 copy.132
  592.5 24.2 %all-to-all-start.5 = ((f32[1,128,32]{2,0,1:T(1,128)}), f32[1,128,32]{2,0,1:T(1,128)S(1)}, u32[]{:S(2)}, u32[]{:S(2)}) async-start(f32[1,128,32]{2,0,1:T(1,128)} %bitcast.95), calls=%async_computation.5 | async-start | bytes 131072 | tf_op jit(solution)/shard_map/all_to_all | solution.py:140
  616.7 0.7 copy.89
  617.4 9.2 %all-to-all-done.5 = f32[1,128,32]{2,0,1:T(1,128)S(1)} async-done(((f32[1,128,32]{2,0,1:T(1,128)}), f32[1,128,32]{2,0,1:T(1,128)S(1)}, u32[]{:S(2)}, u32[]{:S(2)}) %all-to-all-start.5) | async-done | bytes 16416 | tf_op jit(solution)/shard_map/all_to_all | solution.py:140
  626.6 4.4 all-to-all-start.4
  631.0 5.3 broadcast_in_dim.172
  636.3 4.5 all-to-all-done.4
  640.9 5.9 all-to-all-start.3
  647.1 50.9 %all-to-all-done.3 = f32[1,128,4096]{2,0,1:T(1,128)S(1)} async-done(((f32[1,128,4096]{2,0,1:T(1,128)}), f32[1,128,4096]{2,0,1:T(1,128)S(1)}, u32[]{:S(2)}, u32[]{:S(2)}) %all-to-all-start.3) | async-done | bytes 2097184 | tf_op jit(solution)/shard_map/all_to_all | solution.py:141
  698.6 4.3 multiply_reduce_fusion
  703.6 79.3 %all-gather.20.cloned.1.call-done = bf16[64,2,4096]{2,1,0:T(2,128)(2,1)} async-done(((bf16[1,2,4096]{2,1,0:T(2,128)(2,1)}), bf16[64,2,4096]{2,1,0:T(2,128)(2,1)}) %all-gather.20.cloned.1.call-update) | async-done | bytes 1048592 | tf_op jit(solution)/shard_map/all_gather | solution.py:145
  782.9 1.5 reshape.192
  (93 shorter events, 13.9 us)
Async XLA Ops:
  6.5 89.4 %copy-start = (bf16[1,8192,80]{1,2,0:T(8,128)(2,1)S(1)}, bf16[1,8192,80]{1,2,0:T(8,128)(2,1)}, u32[]{:S(2)}) copy-start(bf16[1,8192,80]{1,2,0:T(8,128)(2,1)} %param.27) | copy-start | bytes 3932164
  6.5 89.4 %copy-start.27 = (f32[1,8192]{1,0:T(1,128)S(1)}, f32[1,8192]{1,0:T(1,128)}, u32[]{:S(2)}) copy-start(f32[1,8192]{1,0:T(1,128)} %param.26) | copy-start | bytes 98308
  6.5 87.1 %all-gather.16.cloned.1.call-start = ((), (), s32[]{:S(2)}) async-start(), calls=%async_computation.9 | async-start | bytes 2129920 | tf_op jit(solution)/shard_map/all_gather | solution.py:113
  7.3 172.0 %all-gather.10.cloned.1.call-start = ((), (), s32[]{:S(2)}) async-start(), calls=%async_computation.6 | async-start | bytes 1331200 | tf_op jit(solution)/shard_map/all_gather | solution.py:121
  93.7 2.3 copy-start.9
  95.9 1.7 copy-start.13
  95.9 2.9 copy-start.14
  97.6 3.7 copy-start.26
  180.5 1.3 copy-start.2
  208.4 35.6 %all-to-all-start.2 = ((f32[1,128,32]{2,0,1:T(1,128)}), f32[1,128,32]{2,0,1:T(1,128)S(1)}, u32[]{:S(2)}, u32[]{:S(2)}) async-start(f32[1,128,32]{2,0,1:T(1,128)} %bitcast.73), calls=%async_computation.2 | async-start | bytes 131072 | tf_op jit(solution)/shard_map/all_to_all | solution.py:140
  244.0 9.8 %copy-start.16 = (f32[1,128,32]{2,0,1:T(1,128)}, f32[1,128,32]{2,0,1:T(1,128)S(1)}, u32[]{:S(2)}) copy-start(f32[1,128,32]{2,0,1:T(1,128)S(1)} %all-to-all-done.2) | copy-start | bytes 49156
  244.0 14.3 %all-to-all-start.1 = ((f32[1,128,32]{2,0,1:T(1,128)}), f32[1,128,32]{2,0,1:T(1,128)S(1)}, u32[]{:S(2)}, u32[]{:S(2)}) async-start(f32[1,128,32]{2,0,1:T(1,128)} %bitcast.70), calls=%async_computation.1 | async-start | bytes 131072 | tf_op jit(solution)/shard_map/all_to_all | solution.py:139
  258.3 57.1 %all-to-all-start = ((f32[1,128,4096]{2,0,1:T(1,128)}), f32[1,128,4096]{2,0,1:T(1,128)S(1)}, u32[]{:S(2)}, u32[]{:S(2)}) async-start(f32[1,128,4096]{2,0,1:T(1,128)} %broadcast_in_dim.169), calls=%async_computation | async-start | bytes 4194304 | tf_op jit(solution)/shard_map/all_to_all | solution.py:141
  264.2 136.0 %all-gather.18.cloned.1.call-start = ((), (), s32[]{:S(2)}) async-start(), calls=%async_computation.10 | async-start | bytes 1064960 | tf_op jit(solution)/shard_map/all_gather | solution.py:145
  320.3 81.4 %copy-start.7 = (bf16[1,4096,128]{2,1,0:T(8,128)(2,1)S(1)}, bf16[1,4096,128]{2,1,0:T(8,128)(2,1)}, u32[]{:S(2)}) copy-start(bf16[1,4096,128]{2,1,0:T(8,128)(2,1)} %param.28) | copy-start | bytes 3145732
  320.3 81.4 %copy-start.21 = (bf16[1,128,128]{2,1,0:T(8,128)(2,1)S(1)}, bf16[1,128,128]{2,1,0:T(8,128)(2,1)}, u32[]{:S(2)}) copy-start(bf16[1,128,128]{2,1,0:T(8,128)(2,1)} %param.22) | copy-start | bytes 98308
  321.0 85.5 %copy-start.25 = (bf16[1,128,128]{2,1,0:T(8,128)(2,1)S(1)}, bf16[1,128,128]{2,1,0:T(8,128)(2,1)}, u32[]{:S(2)}) copy-start(bf16[1,128,128]{2,1,0:T(8,128)(2,1)} %param.23) | copy-start | bytes 98308
  321.0 164.5 %all-gather.12.cloned.1.call-start = ((), (), s32[]{:S(2)}) async-start(), calls=%async_computation.7 | async-start | bytes 2129920 | tf_op jit(solution)/shard_map/all_gather | solution.py:113
  401.7 86.0 %copy-start.28 = (f32[1,8192]{1,0:T(1,128)S(1)}, f32[1,8192]{1,0:T(1,128)}, u32[]{:S(2)}) copy-start(f32[1,8192]{1,0:T(1,128)} %param.26) | copy-start | bytes 98308
  402.2 87.2 %copy-start.22 = (bf16[128,128]{1,0:T(8,128)(2,1)}, bf16[128,128]{1,0:T(8,128)(2,1)S(1)}, u32[]{:S(2)}) copy-start(bf16[128,128]{1,0:T(8,128)(2,1)S(1)} %fusion.91) | copy-start | bytes 98308
  402.2 4.3 collective-permute-start
  407.1 163.9 %all-gather.14.cloned.1.call-start = ((), (), s32[]{:S(2)}) async-start(), calls=%async_computation.8 | async-start | bytes 1331200 | tf_op jit(solution)/shard_map/all_gather | solution.py:121
  485.5 2.3 copy-start.10
  572.3 1.6 copy-start.24
  592.5 34.1 %all-to-all-start.5 = ((f32[1,128,32]{2,0,1:T(1,128)}), f32[1,128,32]{2,0,1:T(1,128)S(1)}, u32[]{:S(2)}, u32[]{:S(2)}) async-start(f32[1,128,32]{2,0,1:T(1,128)} %bitcast.95), calls=%async_computation.5 | async-start | bytes 131072 | tf_op jit(solution)/shard_map/all_to_all | solution.py:140
  626.6 14.3 %all-to-all-start.4 = ((f32[1,128,32]{2,0,1:T(1,128)}), f32[1,128,32]{2,0,1:T(1,128)S(1)}, u32[]{:S(2)}, u32[]{:S(2)}) async-start(f32[1,128,32]{2,0,1:T(1,128)} %bitcast.92), calls=%async_computation.4 | async-start | bytes 131072 | tf_op jit(solution)/shard_map/all_to_all | solution.py:139
  640.9 57.1 %all-to-all-start.3 = ((f32[1,128,4096]{2,0,1:T(1,128)}), f32[1,128,4096]{2,0,1:T(1,128)S(1)}, u32[]{:S(2)}, u32[]{:S(2)}) async-start(f32[1,128,4096]{2,0,1:T(1,128)} %broadcast_in_dim.172), calls=%async_computation.3 | async-start | bytes 4194304 | tf_op jit(solution)/shard_map/all_to_all | solution.py:141
  646.8 136.1 %all-gather.20.cloned.1.call-start = ((), (), s32[]{:S(2)}) async-start(), calls=%async_computation.11 | async-start | bytes 1064960 | tf_op jit(solution)/shard_map/all_gather | solution.py:145
  702.9 81.5 %copy-start.8 = (bf16[1,4096,128]{2,1,0:T(8,128)(2,1)S(1)}, bf16[1,4096,128]{2,1,0:T(8,128)(2,1)}, u32[]{:S(2)}) copy-start(bf16[1,4096,128]{2,1,0:T(8,128)(2,1)} %param.28) | copy-start | bytes 3145732
  702.9 81.5 %copy-start.15 = (bf16[128,128]{1,0:T(8,128)(2,1)S(1)}, bf16[128,128]{1,0:T(8,128)(2,1)}, u32[]{:S(2)}) copy-start(bf16[128,128]{1,0:T(8,128)(2,1)} %bitcast_select_fusion) | copy-start | bytes 98308
  703.6 81.2 %copy-start.23 = (bf16[128,128]{1,0:T(8,128)(2,1)S(1)}, bf16[128,128]{1,0:T(8,128)(2,1)}, u32[]{:S(2)}) copy-start(bf16[128,128]{1,0:T(8,128)(2,1)} %copy-done.22) | copy-start | bytes 98308
  703.6 81.8 %copy-start.1 = (bf16[1,8192,80]{1,2,0:T(8,128)(2,1)S(1)}, bf16[1,8192,80]{1,2,0:T(8,128)(2,1)}, u32[]{:S(2)}) copy-start(bf16[1,8192,80]{1,2,0:T(8,128)(2,1)} %param.27) | copy-start | bytes 3932164
Sparse Core Ops, SparseCore 0:
  10.5 83.1 all-gather.15
  97.7 81.4 all-gather.9
  321.1 79.0 all-gather.17
  407.2 78.1 all-gather.11
  489.5 81.4 all-gather.13
  703.7 79.1 all-gather.19
where the time goes:
time: 800 us; the launch traced here: 793 us
  waiting for transfers between devices  610 us (76%)
  starting transfers between devices  74.2 us (9%)
  local copies, waits for them, and re-layouts  35 us (4%)
  matrix products  26.5 us (3%)
  other arithmetic  22.1 us (3%)
  between operations  16.8 us (2%)
  loops' own time  8.38 us (1%)
    all_gather x2, waiting for transfers between devices, on_device(): gathered = lax.all_gather(current, 'kv', axis=1, tiled=True)  164 us
    all_gather x2, waiting for transfers between devices, on_device(): lax.all_gather(attended, 'kv', axis=0, tiled=True)  158 us
    all_gather x2, waiting for transfers between devices, on_device(): united = lax.all_gather(local_cols, 'kv', axis=1, tiled=True)  157 us
    all_to_all x2, waiting for transfers between devices, on_device(): lax.all_to_all(partial_value[2][None], 'kv', split_axis=1, concat_axis=0,...  100 us
    all_to_all x2, starting transfers between devices, on_device(): lax.all_to_all(partial_value[1][None], 'kv', split_axis=1, concat_axis=0,...  49.9 us
    all_to_all x2, waiting for transfers between devices, on_device(): lax.all_to_all(partial_value[1][None], 'kv', split_axis=1, concat_axis=0,...  18.3 us
  transfers between devices with their start and end apart: 13, of which 13 were waited for; matrix products, arithmetic and copies ran while one was open for 2% of the time, Pallas kernels for 0%

commit v1 on v0

--- a/solution.py
+++ b/solution.py
@@ -2,10 +2,24 @@
 import jax.numpy as jnp
 from jax import lax
 from jax.sharding import PartitionSpec as P
+from jax.lax import all_to_all, axis_size
 
 HD = 128
 HEADS_Q = 32
 KV_HEADS = 4
+
+
+def sheets_clear(slab_in):
+    net_axis = "kv"
+    full_n = axis_size(net_axis)
+    long_array = all_to_all(
+        jnp.tile(slab_in, list(map(lambda h: full_n if h == 1 else 1, range(slab_in.ndim)))),
+        net_axis,
+        split_axis=1,
+        concat_axis=1,
+        tiled=True,
+    )
+    return long_array
 
 
 def passed_along(block, axis, distance):
@@ -110,7 +124,7 @@
             block_starts[jnp.maximum(anchor, 0)],
             fresh_starts[jnp.clip(-anchor - 1, 0, tick_count - 2)],
         )
-        gathered = lax.all_gather(current, "kv", axis=1, tiled=True)
+        gathered = sheets_clear(current)
         wide = gathered.astype(jnp.float32)
         normed = (
             wide * lax.rsqrt(jnp.mean(wide * wide, axis=1, keepdims=True) + 1e-05) * gain

time: 800 us -> 765 us (0.956)
  waiting for transfers between devices: 610 us -> 445 us
  blocking collectives: 0 us -> 122 us
  local copies, waits for them, and re-layouts: 35 us -> 43.3 us
    all_gather x2 -> x0, waiting for transfers between devices: 164 us -> none  [on_device(): gathered = lax.all_gather(current, 'kv', axis=1, tiled=True)]
    all_to_all x0 -> x2, blocking collectives: none -> 122 us  [sheets_clear(): all_to_all(jnp.tile(slab_in, list(map(lambda h: full_n if h == 1 else 1,...]
  transfers between devices with their start and end apart: 13 -> 11, of which waited for: 13 -> 11; matrix products, arithmetic and copies ran while one was open for 2% -> 2% of each run, Pallas kernels for 0% -> 0%
where the time goes in v1:
time: 765 us; the launch traced here: 756 us
  waiting for transfers between devices  445 us (58%)
  blocking collectives  122 us (16%)
  starting transfers between devices  73 us (10%)
  local copies, waits for them, and re-layouts  43.3 us (6%)
  matrix products  25.5 us (3%)
  other arithmetic  22.2 us (3%)
  between operations  16.5 us (2%)
  loops' own time  9.15 us (1%)
    all_gather x2, waiting for transfers between devices, on_device(): lax.all_gather(attended, 'kv', axis=0, tiled=True)  158 us
    all_gather x2, waiting for transfers between devices, on_device(): united = lax.all_gather(local_cols, 'kv', axis=1, tiled=True)  157 us
    all_to_all x2, blocking collectives, sheets_clear(): all_to_all(jnp.tile(slab_in, list(map(lambda h: full_n if h == 1 else 1,...  122 us
    all_to_all x2, waiting for transfers between devices, on_device(): lax.all_to_all(partial_value[2][None], 'kv', split_axis=1, concat_axis=0,...  100 us
    all_to_all x2, starting transfers between devices, on_device(): lax.all_to_all(partial_value[1][None], 'kv', split_axis=1, concat_axis=0,...  49 us
    all_to_all x2, waiting for transfers between devices, on_device(): lax.all_to_all(partial_value[1][None], 'kv', split_axis=1, concat_axis=0,...  18.3 us
  transfers between devices with their start and end apart: 11, of which 11 were waited for; matrix products, arithmetic and copies ran while one was open for 2% of the time, Pallas kernels for 0%

profile of v1, /device:TPU:1, one launch (start us, length us, event | category | flops | bytes accessed | tf_op | source)
XLA Modules:
  0.0 756.3 jit_solution(7747614661823505975)
XLA Ops:
  6.5 1.4 tile.4
  7.9 62.7 %all_to_all.84 = bf16[128,64,128]{2,0,1:T(8,128)(2,1)} all-to-all(bf16[128,64,128]{2,0,1:T(8,128)(2,1)S(1)} %tile.4), channel_id=1, replica_groups=mesh['section'=8,'kv'=64] {'kv'}, dimensions={1} | all-to-all | bytes 4194304 | tf_op jit(solution)/shard_map/all_to_all | solution.py:15
  70.6 3.2 copy.105
  73.9 1.1 fusion.74
  75.0 1.5 fusion.76
  76.5 1.2 fusion.88
  77.9 0.9 copy.109
  83.7 76.3 %all-gather.7.cloned.1.call-done = bf16[128,5120]{0,1:T(8,128)(2,1)} async-done(((bf16[128,80]{0,1:T(8,128)(2,1)}), bf16[128,5120]{0,1:T(8,128)(2,1)}) %all-gather.7.cloned.1.call-update) | async-done | bytes 1310736 | tf_op jit(solution)/shard_map/all_gather | solution.py:135
  160.0 1.3 slice.24
  161.3 1.3 copy.106
  162.9 13.4 %while.58 = (s32[]{:T(128)}, f32[4,128,8]{1,2,0:T(8,128)S(1)}, f32[4,128,8]{1,2,0:T(8,128)S(1)}, f32[4,128,8,128]{3,1,2,0:T(8,128)S(1)}, bf16[4,128,8,128]{3,1,2...) while((s32[]{:T(128)}, f32[4,128,8]{1,2,0:T(8,128)S(1)}, ...), condition=%wide.region_4.5_spmd.clone, body=%wide.region_1.4_spmd.clone.sunk | while | flops 204863488 | bytes 5737833 | solution.py:58
  162.9 1.5 select_reduce_fusion.8
  164.9 1.3 fusion.133
  166.3 1.5 select_reduce_fusion.8
  168.3 1.3 fusion.133
  169.6 1.5 select_reduce_fusion.8
  171.6 1.3 fusion.133
  173.0 1.5 select_reduce_fusion.8
  175.0 1.3 fusion.133
  176.3 12.8 %conditional.2 = (f32[128,32]{0,1:T(8,128)S(1)}, f32[128,32]{0,1:T(8,128)S(1)}, f32[128,4096]{1,0:T(8,128)}) conditional(s32[]{:T(128)} %convert_element_type.63, (f32[128,4,8,128]{3,0,2,1:T(8,128)S(1)}, f32[128,32]{0,1:T(8,128)S(1)}, f32[128,32]{0,1:T(8,128)S(1)}) %tuple.196, (bf16[128,4096]{0,1:T(8,128)(2,1)}, bf16[128,5120]{0,1:T(8,128)(2,1)}, ...), branch_computations={%region_5.6_spmd, %region_6.11_spmd} | conditional | flops 69883904 | bytes 51759524 | solution.py:151
  176.4 1.2 copy.111
  177.6 2.9 copy.163
  189.9 24.9 %all-to-all-start.3 = ((f32[1,128,32]{2,0,1:T(1,128)}), f32[1,128,32]{2,0,1:T(1,128)S(1)}, u32[]{:S(2)}, u32[]{:S(2)}) async-start(f32[1,128,32]{2,0,1:T(1,128)} %bitcast.72), calls=%async_computation.3 | async-start | bytes 131072 | tf_op jit(solution)/shard_map/all_to_all | solution.py:154
  215.5 9.2 %all-to-all-done.3 = f32[1,128,32]{2,0,1:T(1,128)S(1)} async-done(((f32[1,128,32]{2,0,1:T(1,128)}), f32[1,128,32]{2,0,1:T(1,128)S(1)}, u32[]{:S(2)}, u32[]{:S(2)}) %all-to-all-start.3) | async-done | bytes 16416 | tf_op jit(solution)/shard_map/all_to_all | solution.py:154
  224.7 4.4 all-to-all-start.2
  229.1 5.3 broadcast_in_dim.169
  234.4 4.5 all-to-all-done.2
  239.0 5.9 all-to-all-start.1
  246.6 49.5 %all-to-all-done.1 = f32[1,128,4096]{2,0,1:T(1,128)S(1)} async-done(((f32[1,128,4096]{2,0,1:T(1,128)}), f32[1,128,4096]{2,0,1:T(1,128)S(1)}, u32[]{:S(2)}, u32[]{:S(2)}) %all-to-all-start.1) | async-done | bytes 2097184 | tf_op jit(solution)/shard_map/all_to_all | solution.py:155
  296.7 4.3 multiply_reduce_fusion.1
  301.7 79.2 %all-gather.11.cloned.1.call-done = bf16[64,2,4096]{2,1,0:T(2,128)(2,1)} async-done(((bf16[1,2,4096]{2,1,0:T(2,128)(2,1)}), bf16[64,2,4096]{2,1,0:T(2,128)(2,1)}) %all-gather.11.cloned.1.call-update) | async-done | bytes 1048592 | tf_op jit(solution)/shard_map/all_gather | solution.py:159
  380.9 1.5 reshape.223
  382.9 3.3 collective-permute-start
  386.2 1.0 collective-permute-done
  387.8 59.0 %all_to_all.85 = bf16[128,64,128]{2,0,1:T(8,128)(2,1)} all-to-all(bf16[128,64,128]{2,0,1:T(8,128)(2,1)S(1)} %tile.5), channel_id=1, replica_groups=mesh['section'=8,'kv'=64] {'kv'}, dimensions={1} | all-to-all | bytes 4194304 | tf_op jit(solution)/shard_map/all_to_all | solution.py:15
  446.8 3.2 copy.115
  450.1 1.1 fusion.77
  451.2 1.5 fusion.79
  452.6 1.2 fusion.85
  453.8 81.2 %all-gather.9.cloned.1.call-done = bf16[128,5120]{0,1:T(8,128)(2,1)} async-done(((bf16[128,80]{0,1:T(8,128)(2,1)}), bf16[128,5120]{0,1:T(8,128)(2,1)}) %all-gather.9.cloned.1.call-update) | async-done | bytes 1310736 | tf_op jit(solution)/shard_map/all_gather | solution.py:135
  535.0 1.3 slice.25
  536.3 1.3 copy.116
  537.9 13.5 %while.59 = (s32[]{:T(128)}, f32[4,128,8]{1,2,0:T(8,128)S(1)}, f32[4,128,8]{1,2,0:T(8,128)S(1)}, f32[4,128,8,128]{3,1,2,0:T(8,128)S(1)}, bf16[4,128,8,128]{3,1,2...) while((s32[]{:T(128)}, f32[4,128,8]{1,2,0:T(8,128)S(1)}, ...), condition=%wide.region_18.19_spmd.clone, body=%wide.region_15.18_spmd.clone.sunk | while | flops 204863488 | bytes 5737833 | solution.py:58
  537.9 1.5 select_reduce_fusion.9
  540.0 1.3 fusion.137
  541.3 1.5 select_reduce_fusion.9
  543.3 1.3 fusion.137
  544.7 1.5 select_reduce_fusion.9
  546.7 1.3 fusion.137
  548.0 1.5 select_reduce_fusion.9
  550.1 1.3 fusion.137
  551.4 4.4 conditional.3
  551.4 1.2 copy.119
  552.6 2.9 copy.164
  556.5 24.1 %all-to-all-start.7 = ((f32[1,128,32]{2,0,1:T(1,128)}), f32[1,128,32]{2,0,1:T(1,128)S(1)}, u32[]{:S(2)}, u32[]{:S(2)}) async-start(f32[1,128,32]{2,0,1:T(1,128)} %bitcast.95), calls=%async_computation.7 | async-start | bytes 131072 | tf_op jit(solution)/shard_map/all_to_all | solution.py:154
  581.4 9.2 %all-to-all-done.7 = f32[1,128,32]{2,0,1:T(1,128)S(1)} async-done(((f32[1,128,32]{2,0,1:T(1,128)}), f32[1,128,32]{2,0,1:T(1,128)S(1)}, u32[]{:S(2)}, u32[]{:S(2)}) %all-to-all-start.7) | async-done | bytes 16416 | tf_op jit(solution)/shard_map/all_to_all | solution.py:154
  590.5 4.4 all-to-all-start.6
  595.0 5.3 broadcast_in_dim.172
  600.3 4.5 all-to-all-done.6
  604.8 5.9 all-to-all-start.5
  611.0 50.9 %all-to-all-done.5 = f32[1,128,4096]{2,0,1:T(1,128)S(1)} async-done(((f32[1,128,4096]{2,0,1:T(1,128)}), f32[1,128,4096]{2,0,1:T(1,128)S(1)}, u32[]{:S(2)}, u32[]{:S(2)}) %all-to-all-start.5) | async-done | bytes 2097184 | tf_op jit(solution)/shard_map/all_to_all | solution.py:155
  662.5 4.3 multiply_reduce_fusion
  667.5 79.3 %all-gather.13.cloned.1.call-done = bf16[64,2,4096]{2,1,0:T(2,128)(2,1)} async-done(((bf16[1,2,4096]{2,1,0:T(2,128)(2,1)}), bf16[64,2,4096]{2,1,0:T(2,128)(2,1)}) %all-gather.13.cloned.1.call-update) | async-done | bytes 1048592 | tf_op jit(solution)/shard_map/all_gather | solution.py:159
  746.8 1.5 reshape.225
  (93 shorter events, 17.0 us)
Async XLA Ops:
  6.5 69.9 %copy-start = (bf16[1,8192,80]{1,2,0:T(8,128)(2,1)S(1)}, bf16[1,8192,80]{1,2,0:T(8,128)(2,1)}, u32[]{:S(2)}) copy-start(bf16[1,8192,80]{1,2,0:T(8,128)(2,1)} %param.27) | copy-start | bytes 3932164
  6.5 153.5 %all-gather.7.cloned.1.call-start = ((), (), s32[]{:S(2)}) async-start(), calls=%async_computation.8 | async-start | bytes 1331200 | tf_op jit(solution)/shard_map/all_gather | solution.py:135
  73.8 1.1 copy-start.21
  76.4 1.2 copy-start.11
  76.5 2.4 copy-start.12
  77.6 3.6 copy-start.27
  161.3 1.4 copy-start.2
  189.9 34.8 %all-to-all-start.3 = ((f32[1,128,32]{2,0,1:T(1,128)}), f32[1,128,32]{2,0,1:T(1,128)S(1)}, u32[]{:S(2)}, u32[]{:S(2)}) async-start(f32[1,128,32]{2,0,1:T(1,128)} %bitcast.72), calls=%async_computation.3 | async-start | bytes 131072 | tf_op jit(solution)/shard_map/all_to_all | solution.py:154
  224.7 9.7 %copy-start.15 = (f32[1,128,32]{2,0,1:T(1,128)}, f32[1,128,32]{2,0,1:T(1,128)S(1)}, u32[]{:S(2)}) copy-start(f32[1,128,32]{2,0,1:T(1,128)S(1)} %all-to-all-done.3) | copy-start | bytes 49156
  224.7 14.3 %all-to-all-start.2 = ((f32[1,128,32]{2,0,1:T(1,128)}), f32[1,128,32]{2,0,1:T(1,128)S(1)}, u32[]{:S(2)}, u32[]{:S(2)}) async-start(f32[1,128,32]{2,0,1:T(1,128)} %bitcast.69), calls=%async_computation.2 | async-start | bytes 131072 | tf_op jit(solution)/shard_map/all_to_all | solution.py:153
  239.0 57.1 %all-to-all-start.1 = ((f32[1,128,4096]{2,0,1:T(1,128)}), f32[1,128,4096]{2,0,1:T(1,128)S(1)}, u32[]{:S(2)}, u32[]{:S(2)}) async-start(f32[1,128,4096]{2,0,1:T(1,128)} %broadcast_in_dim.169), calls=%async_computation.1 | async-start | bytes 4194304 | tf_op jit(solution)/shard_map/all_to_all | solution.py:155
  244.9 136.1 %all-gather.11.cloned.1.call-start = ((), (), s32[]{:S(2)}) async-start(), calls=%async_computation.10 | async-start | bytes 1064960 | tf_op jit(solution)/shard_map/all_gather | solution.py:159
  301.0 81.5 %copy-start.7 = (bf16[1,4096,128]{2,1,0:T(8,128)(2,1)S(1)}, bf16[1,4096,128]{2,1,0:T(8,128)(2,1)}, u32[]{:S(2)}) copy-start(bf16[1,4096,128]{2,1,0:T(8,128)(2,1)} %param.28) | copy-start | bytes 3145732
  301.0 81.5 %copy-start.20 = (bf16[1,128,128]{2,1,0:T(8,128)(2,1)S(1)}, bf16[1,128,128]{2,1,0:T(8,128)(2,1)}, u32[]{:S(2)}) copy-start(bf16[1,128,128]{2,1,0:T(8,128)(2,1)} %param.22) | copy-start | bytes 98308
  301.7 85.5 %copy-start.26 = (bf16[1,128,128]{2,1,0:T(8,128)(2,1)S(1)}, bf16[1,128,128]{2,1,0:T(8,128)(2,1)}, u32[]{:S(2)}) copy-start(bf16[1,128,128]{2,1,0:T(8,128)(2,1)} %param.23) | copy-start | bytes 98308
  301.7 233.4 %all-gather.9.cloned.1.call-start = ((), (), s32[]{:S(2)}) async-start(), calls=%async_computation.9 | async-start | bytes 1331200 | tf_op jit(solution)/shard_map/all_gather | solution.py:135
  382.9 64.0 %copy-start.23 = (bf16[128,128]{1,0:T(8,128)(2,1)}, bf16[128,128]{1,0:T(8,128)(2,1)S(1)}, u32[]{:S(2)}) copy-start(bf16[128,128]{1,0:T(8,128)(2,1)S(1)} %fusion.84) | copy-start | bytes 98308
  382.9 4.3 collective-permute-start
  387.2 0.6 copy-start.13
  450.1 1.1 copy-start.22
  536.3 1.6 copy-start.25
  556.5 34.0 %all-to-all-start.7 = ((f32[1,128,32]{2,0,1:T(1,128)}), f32[1,128,32]{2,0,1:T(1,128)S(1)}, u32[]{:S(2)}, u32[]{:S(2)}) async-start(f32[1,128,32]{2,0,1:T(1,128)} %bitcast.95), calls=%async_computation.7 | async-start | bytes 131072 | tf_op jit(solution)/shard_map/all_to_all | solution.py:154
  590.5 14.3 %all-to-all-start.6 = ((f32[1,128,32]{2,0,1:T(1,128)}), f32[1,128,32]{2,0,1:T(1,128)S(1)}, u32[]{:S(2)}, u32[]{:S(2)}) async-start(f32[1,128,32]{2,0,1:T(1,128)} %bitcast.92), calls=%async_computation.6 | async-start | bytes 131072 | tf_op jit(solution)/shard_map/all_to_all | solution.py:153
  604.8 57.1 %all-to-all-start.5 = ((f32[1,128,4096]{2,0,1:T(1,128)}), f32[1,128,4096]{2,0,1:T(1,128)S(1)}, u32[]{:S(2)}, u32[]{:S(2)}) async-start(f32[1,128,4096]{2,0,1:T(1,128)} %broadcast_in_dim.172), calls=%async_computation.5 | async-start | bytes 4194304 | tf_op jit(solution)/shard_map/all_to_all | solution.py:155
  610.7 136.1 %all-gather.13.cloned.1.call-start = ((), (), s32[]{:S(2)}) async-start(), calls=%async_computation.11 | async-start | bytes 1064960 | tf_op jit(solution)/shard_map/all_gather | solution.py:159
  666.8 81.4 %copy-start.8 = (bf16[1,4096,128]{2,1,0:T(8,128)(2,1)S(1)}, bf16[1,4096,128]{2,1,0:T(8,128)(2,1)}, u32[]{:S(2)}) copy-start(bf16[1,4096,128]{2,1,0:T(8,128)(2,1)} %param.28) | copy-start | bytes 3145732
  666.8 81.4 %copy-start.14 = (bf16[128,128]{1,0:T(8,128)(2,1)S(1)}, bf16[128,128]{1,0:T(8,128)(2,1)}, u32[]{:S(2)}) copy-start(bf16[128,128]{1,0:T(8,128)(2,1)} %copy-done.13) | copy-start | bytes 98308
  667.5 81.2 %copy-start.24 = (bf16[128,128]{1,0:T(8,128)(2,1)S(1)}, bf16[128,128]{1,0:T(8,128)(2,1)}, u32[]{:S(2)}) copy-start(bf16[128,128]{1,0:T(8,128)(2,1)} %copy-done.23) | copy-start | bytes 98308
  667.5 81.8 %copy-start.1 = (bf16[1,8192,80]{1,2,0:T(8,128)(2,1)S(1)}, bf16[1,8192,80]{1,2,0:T(8,128)(2,1)}, u32[]{:S(2)}) copy-start(bf16[1,8192,80]{1,2,0:T(8,128)(2,1)} %param.27) | copy-start | bytes 3932164
Sparse Core Ops, SparseCore 0:
  77.8 82.1 all-gather.6
  301.8 79.1 all-gather.10
  454.0 81.0 all-gather.8
  667.6 79.1 all-gather.12
